TPU v7x, 256 devices: a whole 4x4x8 slice. The times are simulated.
256 devices in a mesh: section: 4 (over y), expert: 64 (over x, z, core).
Axes of the slice: x: 4, y: 4, z: 8, core: 2. Of those that a mesh axis runs over, the one named last changes fastest.
Arguments:
- tokens: bfloat16 [1024, 4096], P('expert', 'section'), may hold values from -6 to 6
- cotangent: bfloat16 [1024, 4096], P('expert', 'section'), may hold values from -6 to 6
- routes: int32 [1024, 2], P('expert'), may hold values from 0 to 7, all different within a row; in each aligned block of 16 rows (0 to 15, 16 to 31, ...) at most 6 rows name the same one
- w_router: bfloat16 [4096, 8], P('section'), may hold values from -0.09375 to 0.09375
- w_gate: bfloat16 [64, 4096, 1024], P('expert', None, 'section'), may hold values from -0.09375 to 0.09375
- w_up: bfloat16 [64, 4096, 1024], P('expert', None, 'section'), may hold values from -0.09375 to 0.09375
- w_down: bfloat16 [64, 1024, 4096], P('expert', 'section'), may hold values from -0.0625 to 0.0625
Outputs:
- mixed: bfloat16 [1024, 4096], P('expert', 'section')
- grad_tokens: bfloat16 [1024, 4096], P('expert', 'section')
- grad_router: float32 [4096, 8], P('section')
- grad_gate: bfloat16 [64, 4096, 1024], P('expert', None, 'section')
- grad_up: bfloat16 [64, 4096, 1024], P('expert', None, 'section')
- grad_down: bfloat16 [64, 1024, 4096], P('expert', 'section')
Inputs may be any that keep to these rules, and one draw needn't show every extreme that they name: `routes`: each token names two different experts. Within each aligned block of 16 tokens no expert is named by more than 6 tokens, and in every draw some block has an expert named by exactly 6 tokens.
All inputs are finite; a program needn't handle non-finite values.
Results may differ from a plain program's by a relative error of at most 0.023.
Values may be sent and summed in bfloat16 or wider, within the bound.
No kernel may reach another device: no remote copies, remote signals or barrier semaphores. Data moves between devices by JAX's collectives and lax.ppermute only.
A program may use at most 128 MiB of HBM per device.

v0:
```python
import jax
import jax.numpy as jnp
import numpy as np
from jax import lax
from jax.sharding import Mesh
from jax.sharding import PartitionSpec as P

CAP = 6
LANES = 128
EXPERT_AXES = ("ex", "ez", "ec")


def expert_size():
    size = 1
    for name in EXPERT_AXES:
        size = size * lax.axis_size(name)
    return size


def per_device(tokens, cotangent, routes, w_router, w_gate, w_up, w_down):
    highest = lax.Precision.HIGHEST
    experts = w_router.shape[1]
    groups = expert_size() // experts
    capacity = CAP
    tok_count, width = tokens.shape
    n_section = lax.axis_size("section")
    slot_total = experts * capacity
    route_hot = routes[:, :, None] == jnp.arange(experts, dtype=jnp.int32)[None, None, :]
    zero_f = jnp.zeros((), jnp.float32)
    counts_flat = route_hot.astype(jnp.int32).reshape(2 * tok_count, experts)
    earlier = jnp.cumsum(counts_flat, axis=0) - counts_flat
    position = jnp.sum(earlier * counts_flat, axis=1).reshape(tok_count, 2)
    slot_row = routes * capacity + position
    slot_ids = jnp.arange(slot_total, dtype=jnp.int32)[None, :]
    pick_first = slot_row[:, 0:1] == slot_ids
    pick_second = slot_row[:, 1:2] == slot_ids
    pick_both = (pick_first | pick_second).astype(jnp.bfloat16)
    x_source = jnp.einsum(
        "ts,td->sd", pick_both, tokens, preferred_element_type=jnp.float32
    ).astype(jnp.bfloat16)
    zero_i = jnp.zeros((), jnp.int32)
    other_slot = jnp.sum(
        jnp.where(pick_first, routes[:, 1:2], zero_i)
        + jnp.where(pick_second, routes[:, 0:1], zero_i),
        axis=0,
    )
    half = capacity * width // LANES
    meta = jnp.zeros((experts, 16, LANES), jnp.bfloat16)
    meta = meta.at[:, 0, :capacity].set(other_slot.reshape(experts, capacity).astype(jnp.bfloat16))

    def spread(block):
        rows = block.shape[1]
        return jnp.broadcast_to(block[:, None], (experts, groups, rows, LANES)).reshape(
            experts * groups, rows, LANES
        )

    x_block = x_source.reshape(experts, half, LANES)
    x_recv = lax.all_to_all(spread(x_block), EXPERT_AXES, 0, 0, tiled=True)
    cot_source = jnp.einsum(
        "ts,td->sd", pick_both, cotangent, preferred_element_type=jnp.float32
    ).astype(jnp.bfloat16)
    c_block = jnp.concatenate([cot_source.reshape(experts, half, LANES), meta], axis=1)
    row_total = x_recv.shape[0] * capacity
    x_recv = x_recv.reshape(row_total, width)
    x_rows = lax.all_gather(x_recv, "section", axis=1, tiled=True)
    c_block, x_recv = lax.optimization_barrier((c_block, x_recv))
    c_recv = lax.all_to_all(spread(c_block), EXPERT_AXES, 0, 0, tiled=True)
    cot_recv = c_recv[:, :half].reshape(row_total, width)
    other_recv = c_recv[:, half, :capacity].astype(jnp.int32).reshape(row_total)
    w_router, x_recv = lax.optimization_barrier((w_router, x_recv))
    partial_logits = jnp.dot(tokens, w_router, preferred_element_type=jnp.float32)
    logits = lax.psum(partial_logits, "section")
    chosen = jnp.sum(jnp.where(route_hot, logits[:, None, :], zero_f), axis=2)
    gate_first = 1.0 / (1.0 + jnp.exp(chosen[:, 1] - chosen[:, 0]))
    gate_second = 1.0 / (1.0 + jnp.exp(chosen[:, 0] - chosen[:, 1]))
    cot_float = cotangent.astype(jnp.float32)
    row_logits = lax.psum(jnp.dot(x_recv, w_router, preferred_element_type=jnp.float32), "section")
    own = lax.axis_index(EXPERT_AXES) // groups
    expert_ids = jnp.arange(experts, dtype=jnp.int32)[None, :]
    own_logit = jnp.sum(jnp.where(expert_ids == own, row_logits, zero_f), axis=1)
    other_logit = jnp.sum(jnp.where(expert_ids == other_recv[:, None], row_logits, zero_f), axis=1)
    row_gate = 1.0 / (1.0 + jnp.exp(other_logit - own_logit))
    gate_local = w_gate[0]
    up_local = w_up[0]
    down_local = w_down[0]
    pre_gate = jnp.dot(x_rows, gate_local, preferred_element_type=jnp.float32)
    pre_up = jnp.dot(x_rows, up_local, preferred_element_type=jnp.float32)
    sigmoid_gate = jax.nn.sigmoid(pre_gate)
    activated = pre_gate * sigmoid_gate
    hidden = (activated * pre_up).astype(jnp.bfloat16)
    hid = gate_local.shape[1]
    down_blocks = down_local.reshape(hid, n_section, width)
    gate_blocks = gate_local.reshape(n_section, width, hid)
    up_blocks = up_local.reshape(n_section, width, hid)
    out_piece = jnp.einsum("pf,fsd->spd", hidden, down_blocks, preferred_element_type=jnp.float32)
    out_piece = out_piece.astype(jnp.bfloat16).reshape(n_section * row_total, width)
    out_red = lax.psum_scatter(out_piece, "section", scatter_dimension=0, tiled=True)
    out_red, cot_recv, row_gate, gate_first, gate_second = lax.optimization_barrier(
        (out_red, cot_recv, row_gate, gate_first, gate_second)
    )
    cot_rows = lax.all_gather(cot_recv, "section", axis=1, tiled=True)
    dy_rows = (row_gate[:, None] * cot_rows.astype(jnp.float32)).astype(jnp.bfloat16)
    n_dev = row_total // capacity
    out_back = lax.all_to_all(out_red.reshape(n_dev, half, LANES), EXPERT_AXES, 0, 0, tiled=True)
    out_back = out_back.reshape(experts, groups, half, LANES).astype(jnp.float32)
    slot_out = jnp.sum(out_back, axis=1).reshape(slot_total, width)
    d_hidden = jnp.einsum("pd,fd->pf", dy_rows, down_local, preferred_element_type=jnp.float32)
    grad_down = jnp.einsum("pf,pd->fd", hidden, dy_rows, preferred_element_type=jnp.float32).astype(
        jnp.bfloat16
    )
    d_pre_gate = (
        d_hidden * pre_up * sigmoid_gate * (1.0 + pre_gate * (1.0 - sigmoid_gate))
    ).astype(jnp.bfloat16)
    d_pre_up = (d_hidden * activated).astype(jnp.bfloat16)
    grad_gate = jnp.einsum(
        "pd,pf->df", x_rows, d_pre_gate, preferred_element_type=jnp.float32
    ).astype(jnp.bfloat16)
    grad_up = jnp.einsum("pd,pf->df", x_rows, d_pre_up, preferred_element_type=jnp.float32).astype(
        jnp.bfloat16
    )
    first_float = pick_first.astype(jnp.float32)
    second_float = pick_second.astype(jnp.float32)
    out_first = jnp.dot(first_float, slot_out, precision=highest)
    out_second = jnp.dot(second_float, slot_out, precision=highest)
    mixed = (gate_first[:, None] * out_first + gate_second[:, None] * out_second).astype(
        jnp.bfloat16
    )
    local_inner = jnp.stack(
        [jnp.sum(cot_float * out_first, axis=1), jnp.sum(cot_float * out_second, axis=1)], axis=1
    )
    dx_piece = jnp.einsum(
        "pf,sdf->spd", d_pre_gate, gate_blocks, preferred_element_type=jnp.float32
    )
    dx_piece = dx_piece + jnp.einsum(
        "pf,sdf->spd", d_pre_up, up_blocks, preferred_element_type=jnp.float32
    )
    gate_inner = lax.psum(local_inner, "section")
    d_first = gate_first * gate_second * (gate_inner[:, 0] - gate_inner[:, 1])
    d_logits = jnp.where(route_hot[:, 0, :], d_first[:, None], zero_f) - jnp.where(
        route_hot[:, 1, :], d_first[:, None], zero_f
    )
    dx_piece = dx_piece.astype(jnp.bfloat16).reshape(n_section * row_total, width)
    d_logits, dx_piece = lax.optimization_barrier((d_logits, dx_piece))
    dx_red = lax.psum_scatter(dx_piece, "section", scatter_dimension=0, tiled=True)
    router_part = jnp.einsum("te,tf->ef", d_logits, tokens.astype(jnp.float32), precision=highest)
    router_part = lax.psum(router_part, EXPERT_AXES[2])
    for name in (EXPERT_AXES[1], EXPERT_AXES[0]):
        router_part = jnp.sum(lax.all_gather(router_part, name, axis=0), axis=0)
    router_part, dx_red = lax.optimization_barrier((router_part, dx_red))
    dx_back = lax.all_to_all(dx_red.reshape(n_dev, half, LANES), EXPERT_AXES, 0, 0, tiled=True)
    dx_back = dx_back.reshape(experts, groups, half, LANES).astype(jnp.float32)
    slot_dx = jnp.sum(dx_back, axis=1).reshape(slot_total, width)
    dx_expert = jnp.dot(first_float, slot_dx, precision=highest)
    dx_expert = dx_expert + jnp.dot(second_float, slot_dx, precision=highest)
    router_float = w_router.astype(jnp.float32)
    grad_tokens = (dx_expert + jnp.dot(d_logits, router_float.T, precision=highest)).astype(
        jnp.bfloat16
    )
    grad_router = router_part.T
    return (mixed, grad_tokens, grad_router, grad_gate[None], grad_up[None], grad_down[None])


def expert_shape(devices):
    try:
        xs = sorted({d.coords[0] for d in devices.flat})
        zs = sorted({d.coords[2] for d in devices.flat})
        cores = sorted({d.core_on_chip for d in devices.flat})
        shape = (len(xs), len(zs), len(cores))
    except AttributeError:
        shape = (4, 8, 2)
    if int(np.prod(shape)) != devices.shape[1]:
        shape = (devices.shape[1] // 16, 8, 2)
    return shape


def solution(mesh):
    devices = mesh.devices
    fine = Mesh(
        devices.reshape((devices.shape[0],) + expert_shape(devices)), ("section",) + EXPERT_AXES
    )
    ex = EXPERT_AXES
    in_specs = (
        P(ex, "section"),
        P(ex, "section"),
        P(ex, None),
        P("section", None),
        P(ex, None, "section"),
        P(ex, None, "section"),
        P(ex, "section", None),
    )
    out_specs = (
        P(ex, "section"),
        P(ex, "section"),
        P("section", None),
        P(ex, None, "section"),
        P(ex, None, "section"),
        P(ex, "section", None),
    )
    return jax.shard_map(
        per_device, mesh=fine, in_specs=in_specs, out_specs=out_specs, check_vma=False
    )
```

profile of v0, /device:TPU:1, one launch (start us, length us, event | category | flops | bytes accessed | tf_op | source)
XLA Modules:
  0.0 275.1 jit_solution(3696435519088308416)
XLA Ops:
  7.2 0.9 copy.41
  8.3 0.2 select_reduce_fusion
  8.7 0.7 multiply_add_fusion
  9.4 0.8 slice_bitcast_fusion.3
  10.2 1.0 convolution_convert_fusion.5
  11.3 0.1 broadcast_in_dim.98
  11.4 35.8 %all_to_all.20 = bf16[64,48,128]{2,1,0:T(8,128)(2,1)S(1)} all-to-all(bf16[64,48,128]{2,1,0:T(8,128)(2,1)S(1)} %bitcast.102), channel_id=1, replica_groups=mesh['section'=4,'ex'=4,'ez'=8,'ec'=2] {'ex','ez','ec'}, dimensions={0} | all-to-all | bytes 1572864 | tf_op jit(solution)/shard_map/all_to_all | solution.py:58
  47.1 1.2 reshape.137
  48.4 4.5 %reshape_squeeze.9 = bf16[256,4,1024]{2,1,0:T(4,128)(2,1)} reshape(bf16[1,256,4096]{2,1,0:T(8,128)(2,1)} %param.15) | data formatting | bytes 4194304 | tf_op jit(solution)/shard_map/reshape;squeeze | solution.py:92
  52.9 34.7 %all-gather.4.cloned.1.call-done = bf16[384,4096]{1,0:T(8,128)(2,1)} async-done(((bf16[384,1024]{1,0:T(8,128)(2,1)}), bf16[384,4096]{1,0:T(8,128)(2,1)}) %all-gather.4.cloned.1.call-update) | async-done | bytes 3145744 | tf_op jit(solution)/shard_map/all_gather | solution.py:65
  87.6 3.7 %fusion.7 = f32[384,256]{1,0:T(8,128)S(1)} fusion(bf16[384,4096]{1,0:T(8,128)(2,1)} %all-gather.4.cloned.1.call-done, bf16[1,4096,256]{2,1,0:T(8,128)(2,1)} %param.13), kind=kOutput, calls=%fused_computation.13 | convolution fusion | flops 805306368 | bytes 5636096 | tf_op jit(solution)/shard_map/dot_general | solution.py:86
  91.3 1.7 multiply_convert_fusion.5
  93.1 3.4 %convolution_convert_fusion.3 = bf16[384,4,1024]{2,0,1:T(8,128)(2,1)} fusion(bf16[256,4,1024]{2,1,0:T(4,128)(2,1)S(1)} %copy-done.1, bf16[384,256]{1,0:T(8,128)(2,1)S(1)} %get-tuple-element.59), kind=kOutput, calls=%fused_computation.8 | convolution fusion | flops 806879232 | bytes 5439488 | tf_op jit(solution)/shard_map/pf,fsd->spd/dot_general | solution.py:95
  96.7 0.3 convolution_convert_fusion.4
  97.1 1.2 broadcast_in_dim.104
  98.3 10.9 %all-to-all-start.1 = ((bf16[64,64,128]{2,1,0:T(8,128)(2,1)}), bf16[64,64,128]{2,1,0:T(8,128)(2,1)}, u32[]{:S(2)}, u32[]{:S(2)}) async-start(bf16[64,64,128]{2,1,0:T(8,128)(2,1)} %bitcast.101), calls=%async_computation.2 | async-start | bytes 2097152 | tf_op jit(solution)/shard_map/all_to_all | solution.py:67
  109.3 0.1 convolution_bitcast_fusion.1
  109.5 0.3 fusion.36
  109.8 13.5 %all-reduce.1 = (f32[384,8]{0,1:T(8,128)S(1)}, f32[16,8]{0,1:T(8,128)S(1)}) all-reduce(f32[384,8]{0,1:T(8,128)S(1)} %fusion.36, f32[16,8]{0,1:T(8,128)S(1)} %convolution_bitcast_fusion.1), channel_id=1, replica_groups=mesh['section'=4,'ex'=4,'ez'=8,'ec'=2] {'section'}, use_global_device_ids=true, to_apply=%region_4.5 | all-reduce | flops 3200 | bytes 25600 | tf_op jit(solution)/shard_map/psum | solution.py:77
  123.3 14.4 %all-to-all-done.1 = bf16[64,64,128]{2,1,0:T(8,128)(2,1)} async-done(((bf16[64,64,128]{2,1,0:T(8,128)(2,1)}), bf16[64,64,128]{2,1,0:T(8,128)(2,1)}, u32[]{:S(2)}, u32[]{:S(2)}) %all-to-all-start.1) | async-done | bytes 1048608 | tf_op jit(solution)/shard_map/all_to_all | solution.py:67
  137.7 1.0 fusion.20
  138.7 0.1 reshape.147
  138.9 1.2 slice.73
  140.1 1.2 reshape.141
  141.4 2.2 reshape.142
  143.6 7.4 %all-to-all-start.2 = ((bf16[64,48,128]{2,1,0:T(8,128)(2,1)}), bf16[64,48,128]{2,1,0:T(8,128)(2,1)S(1)}, u32[]{:S(2)}, u32[]{:S(2)}) async-start(bf16[64,48,128]{2,1,0:T(8,128)(2,1)} %reshape.142), calls=%async_computation.3 | async-start | bytes 1572864 | tf_op jit(solution)/shard_map/all_to_all | solution.py:104
  151.0 22.9 %all-to-all-done.2 = bf16[64,48,128]{2,1,0:T(8,128)(2,1)S(1)} async-done(((bf16[64,48,128]{2,1,0:T(8,128)(2,1)}), bf16[64,48,128]{2,1,0:T(8,128)(2,1)S(1)}, u32[]{:S(2)}, u32[]{:S(2)}) %all-to-all-start.2) | async-done | bytes 786464 | tf_op jit(solution)/shard_map/all_to_all | solution.py:104
  174.1 0.2 fusion.22
  174.3 1.0 fusion.18
  175.3 7.1 %psum.30 = f32[16,2]{0,1:T(2,128)S(1)} all-reduce(f32[16,2]{0,1:T(2,128)S(1)} %pad_maximum_fusion), channel_id=1, replica_groups=mesh['section'=4,'ex'=4,'ez'=8,'ec'=2] {'section'}, use_global_device_ids=true, to_apply=%region_12.13 | all-reduce | flops 32 | bytes 256 | tf_op jit(solution)/shard_map/psum | solution.py:137
  182.5 3.9 %multiply_convert_fusion.3 = (bf16[384,256]{1,0:T(8,128)(2,1)S(1)}, bf16[384,256]{1,0:T(8,128)(2,1)S(1)}) fusion(f32[384,256]{1,0:T(8,128)} %copy-done.10, f32[384,256]{1,0:T(8,128)} %get-tuple-element.60, bf16[1,256,4096]{2,1,0:T(8,128)(2,1)} %param.15, bf16[384,4096]{1,0:T(8,128)(2,1)} %all-gather.6.cloned.1.call-done, f32[384]{0:T(512)S(1)} %add_divide_fusion.1), kind=kOutput, calls=%fused_computation.25 | convolution fusion | flops 811302912 | bytes 6424064 | tf_op jit(solution)/shard_map/pd,fd->pf/dot_general | solution.py:107
  186.4 1.0 fusion.14
  187.4 2.9 %add_convert_fusion = bf16[384,4,1024]{2,0,1:T(8,128)(2,1)} fusion(f32[384,4,1024]{2,0,1:T(8,128)S(1)} %fusion.14, bf16[4,1024,256]{2,1,0:T(8,128)(2,1)S(1)} %bitcast.98, bf16[384,256]{1,0:T(8,128)(2,1)S(1)} %get-tuple-element.50), kind=kOutput, calls=%fused_computation | convolution fusion | flops 808452096 | bytes 11730944 | tf_op jit(solution)/shard_map/pf,sdf->spd/dot_general | solution.py:134
  190.3 0.1 convolution_bitcast_fusion
  190.4 5.2 %psum.31 = f32[1,8,1024]{2,1,0:T(8,128)S(1)} all-reduce(f32[1,8,1024]{2,1,0:T(8,128)S(1)} %convolution_bitcast_fusion), channel_id=1, replica_groups=mesh['section'=4,'ex'=4,'ez'=8,'ec'=2] {'ec'}, use_global_device_ids=true, to_apply=%region_13.14 | all-reduce | flops 8192 | bytes 65536 | tf_op jit(solution)/shard_map/psum | solution.py:146
  195.7 20.2 %all_gather.21 = f32[8,8,1024]{2,1,0:T(8,128)S(1)} all-gather(f32[1,8,1024]{2,1,0:T(8,128)S(1)} %psum.31), channel_id=1, replica_groups=mesh['section'=4,'ex'=4,'ez'=8,'ec'=2] {'ez'}, dimensions={0}, use_global_device_ids=true | all-gather | bytes 294912 | tf_op jit(solution)/shard_map/all_gather | solution.py:148
  215.8 10.6 %all-gather = f32[32,1024]{1,0:T(8,128)S(1)} all-gather(f32[8,1024]{1,0:T(8,128)S(1)} %reduce_sum.107), channel_id=2, replica_groups=mesh['section'=4,'ex'=4,'ez'=8,'ec'=2] {'ex'}, dimensions={0}, use_global_device_ids=true | all-gather | bytes 163840 | tf_op jit(solution)/shard_map/all_gather | solution.py:148
  226.5 0.6 bitcast_reduce_fusion
  227.1 4.2 %reduce-scatter.5.cloned.1.call-done = bf16[384,1024]{1,0:T(8,128)(2,1)} async-done(((bf16[1536,1024]{1,0:T(8,128)(2,1)}), bf16[384,1024]{1,0:T(8,128)(2,1)}) %reduce-scatter.5.cloned.1.call-update) | async-done | bytes 786448 | tf_op jit(solution)/shard_map/reduce_scatter | solution.py:144
  231.3 2.2 reshape.145
  233.5 10.6 %all-to-all-start.3 = ((bf16[64,48,128]{2,1,0:T(8,128)(2,1)}), bf16[64,48,128]{2,1,0:T(8,128)(2,1)S(1)}, u32[]{:S(2)}, u32[]{:S(2)}) async-start(bf16[64,48,128]{2,1,0:T(8,128)(2,1)} %reshape.145), calls=%async_computation.5 | async-start | bytes 1572864 | tf_op jit(solution)/shard_map/all_to_all | solution.py:150
  244.1 4.7 %fusion.2 = bf16[1,256,4096]{2,1,0:T(8,128)(2,1)} fusion(bf16[384,256]{1,0:T(8,128)(2,1)S(1)} %get-tuple-element.59, bf16[384,4096]{1,0:T(8,128)(2,1)} %all-gather.6.cloned.1.call-done, f32[384]{0:T(512)S(1)} %add_divide_fusion.1), kind=kOutput, calls=%fused_computation.7 | convolution fusion | flops 811073536 | bytes 5441024 | tf_op jit(solution)/shard_map/pf,pd->fd/dot_general | solution.py:108
  248.8 2.6 fusion
  251.4 2.6 fusion.1
  254.1 13.0 %all-to-all-done.3 = bf16[64,48,128]{2,1,0:T(8,128)(2,1)S(1)} async-done(((bf16[64,48,128]{2,1,0:T(8,128)(2,1)}), bf16[64,48,128]{2,1,0:T(8,128)(2,1)S(1)}, u32[]{:S(2)}, u32[]{:S(2)}) %all-to-all-start.3) | async-done | bytes 786464 | tf_op jit(solution)/shard_map/all_to_all | solution.py:150
  267.2 0.2 fusion.24
  267.5 0.2 convolution_add_fusion.1
  267.7 0.8 fusion.10
  (57 shorter events, 1.5 us)
Async XLA Ops:
  7.2 84.1 %copy-start = (bf16[1,4096,256]{2,1,0:T(8,128)(2,1)S(1)}, bf16[1,4096,256]{2,1,0:T(8,128)(2,1)}, u32[]{:S(2)}) copy-start(bf16[1,4096,256]{2,1,0:T(8,128)(2,1)} %param.14) | copy-start | bytes 6291460
  7.2 80.4 %all-gather.4.cloned.1.call-start = ((), (), s32[]{:S(2)}) async-start(), calls=%async_computation.6 | async-start | bytes 3932160 | tf_op jit(solution)/shard_map/all_gather | solution.py:65
  48.4 93.0 %reduce-scatter.3.cloned.1.call-start = ((), (), s32[]{:S(2)}) async-start(), calls=%async_computation.7 | async-start | bytes 3932160 | tf_op jit(solution)/shard_map/reduce_scatter | solution.py:97
  87.6 3.7 %copy-start.8 = (bf16[384,4096]{1,0:T(8,128)(2,1)S(1)}, bf16[384,4096]{1,0:T(8,128)(2,1)}, u32[]{:S(2)}) copy-start(bf16[384,4096]{1,0:T(8,128)(2,1)} %all-gather.4.cloned.1.call-done) | copy-start | bytes 9437188
  91.3 1.8 copy-start.10
  91.3 1.8 copy-start.1
  93.1 3.6 %copy-start.6 = (bf16[16,1024]{1,0:T(8,128)(2,1)S(1)}, bf16[16,1024]{1,0:T(8,128)(2,1)}, u32[]{:S(2)}) copy-start(bf16[16,1024]{1,0:T(8,128)(2,1)} %param.10) | copy-start | bytes 98308
  96.5 12.8 %copy-start.4 = (bf16[16,1024]{1,0:T(8,128)(2,1)S(1)}, bf16[16,1024]{1,0:T(8,128)(2,1)}, u32[]{:S(2)}) copy-start(bf16[16,1024]{1,0:T(8,128)(2,1)} %param.9) | copy-start | bytes 98308
  96.5 12.8 %copy-start.5 = (bf16[1024,8]{0,1:T(8,128)(2,1)S(1)}, bf16[1024,8]{0,1:T(8,128)(2,1)}, u32[]{:S(2)}) copy-start(bf16[1024,8]{0,1:T(8,128)(2,1)} %param.12) | copy-start | bytes 49156
  96.5 13.0 %copy-start.2 = (bf16[384,1024]{1,0:T(8,128)(2,1)S(1)}, bf16[384,1024]{1,0:T(8,128)(2,1)}, u32[]{:S(2)}) copy-start(bf16[384,1024]{1,0:T(8,128)(2,1)} %reshape.137) | copy-start | bytes 2359300
  96.5 26.8 %copy-start.7 = (s32[16,2]{0,1:T(2,128)S(1)}, s32[16,2]{0,1:T(2,128)}, u32[]{:S(2)}) copy-start(s32[16,2]{0,1:T(2,128)} %param.11) | copy-start | bytes 388
  98.3 39.4 %all-to-all-start.1 = ((bf16[64,64,128]{2,1,0:T(8,128)(2,1)}), bf16[64,64,128]{2,1,0:T(8,128)(2,1)}, u32[]{:S(2)}, u32[]{:S(2)}) async-start(bf16[64,64,128]{2,1,0:T(8,128)(2,1)} %bitcast.101), calls=%async_computation.2 | async-start | bytes 2097152 | tf_op jit(solution)/shard_map/all_to_all | solution.py:67
  109.2 73.2 %all-gather.6.cloned.1.call-start = ((), (), s32[]{:S(2)}) async-start(), calls=%async_computation.8 | async-start | bytes 3932160 | tf_op jit(solution)/shard_map/all_gather | solution.py:101
  143.6 30.4 %all-to-all-start.2 = ((bf16[64,48,128]{2,1,0:T(8,128)(2,1)}), bf16[64,48,128]{2,1,0:T(8,128)(2,1)S(1)}, u32[]{:S(2)}, u32[]{:S(2)}) async-start(bf16[64,48,128]{2,1,0:T(8,128)(2,1)} %reshape.142), calls=%async_computation.3 | async-start | bytes 1572864 | tf_op jit(solution)/shard_map/all_to_all | solution.py:104
  151.0 80.4 %reduce-scatter.5.cloned.1.call-start = ((), (), s32[]{:S(2)}) async-start(), calls=%async_computation.9 | async-start | bytes 3932160 | tf_op jit(solution)/shard_map/reduce_scatter | solution.py:144
  182.5 3.9 %copy-start.3 = (bf16[1,4096,256]{2,1,0:T(8,128)(2,1)S(1)}, bf16[1,4096,256]{2,1,0:T(8,128)(2,1)}, u32[]{:S(2)}) copy-start(bf16[1,4096,256]{2,1,0:T(8,128)(2,1)} %param.13) | copy-start | bytes 6291460
  233.5 33.6 %all-to-all-start.3 = ((bf16[64,48,128]{2,1,0:T(8,128)(2,1)}), bf16[64,48,128]{2,1,0:T(8,128)(2,1)S(1)}, u32[]{:S(2)}, u32[]{:S(2)}) async-start(bf16[64,48,128]{2,1,0:T(8,128)(2,1)} %reshape.145), calls=%async_computation.5 | async-start | bytes 1572864 | tf_op jit(solution)/shard_map/all_to_all | solution.py:150
  244.1 4.7 %copy-start.9 = (bf16[384,4096]{1,0:T(8,128)(2,1)S(1)}, bf16[384,4096]{1,0:T(8,128)(2,1)}, u32[]{:S(2)}) copy-start(bf16[384,4096]{1,0:T(8,128)(2,1)} %all-gather.4.cloned.1.call-done) | copy-start | bytes 9437188
Sparse Core Ops, SparseCore 0:
  48.5 39.0 all-gather.3
  96.6 41.3 reduce-scatter.2
  141.5 40.6 all-gather.5
  190.4 40.8 reduce-scatter.4
where the time goes:
time: 276 us; the launch traced here: 275 us
  blocking collectives  92.4 us (33%)
  waiting for transfers between devices  89.4 us (32%)
  matrix products  30.9 us (11%)
  starting transfers between devices  29.1 us (11%)
  local copies, waits for them, and re-layouts  16.1 us (6%)
  between operations  14.1 us (5%)
  other arithmetic  3.15 us (1%)
    all_to_all x1, blocking collectives, per_device(): x_recv = lax.all_to_all(spread(x_block), EXPERT_AXES, 0, 0, tiled=True)  35.8 us
    all_gather x1, waiting for transfers between devices, per_device(): x_rows = lax.all_gather(x_recv, 'section', axis=1, tiled=True)  34.7 us
    all_gather x2, blocking collectives, per_device(): router_part = jnp.sum(lax.all_gather(router_part, name, axis=0), axis=0)  30.8 us
    all_to_all x1, waiting for transfers between devices, per_device(): lax.all_to_all(out_red.reshape(n_dev, half, LANES), EXPERT_AXES, 0, 0, ti...  22.9 us
    all_to_all x1, waiting for transfers between devices, per_device(): c_recv = lax.all_to_all(spread(c_block), EXPERT_AXES, 0, 0, tiled=True)  14.4 us
    psum x1, blocking collectives, per_device(): lax.psum(jnp.dot(x_recv, w_router, preferred_element_type=jnp.float32), '...  13.5 us
    all_to_all x1, waiting for transfers between devices, per_device(): lax.all_to_all(dx_red.reshape(n_dev, half, LANES), EXPERT_AXES, 0, 0, til...  13 us
    all_to_all x1, starting transfers between devices, per_device(): c_recv = lax.all_to_all(spread(c_block), EXPERT_AXES, 0, 0, tiled=True)  10.9 us
  transfers between devices with their start and end apart: 7, of which 5 were waited for; matrix products, arithmetic and copies ran while one was open for 9% of the time, Pallas kernels for 0%

commit v1 on v0

--- a/solution.py
+++ b/solution.py
@@ -62,7 +62,13 @@
     c_block = jnp.concatenate([cot_source.reshape(experts, half, LANES), meta], axis=1)
     row_total = x_recv.shape[0] * capacity
     x_recv = x_recv.reshape(row_total, width)
-    x_rows = lax.all_gather(x_recv, "section", axis=1, tiled=True)
+    peers = lax.axis_size("section")
+    moving, parts = (x_recv, [x_recv])
+    for _ in range(peers - 1):
+        moving = lax.ppermute(moving, "section", [(i, (i + 1) % peers) for i in range(peers)])
+        parts.insert(0, moving)
+    flat = jnp.concatenate(parts, axis=1)
+    x_rows = jnp.roll(flat, (lax.axis_index("section") + 1) * x_recv.shape[1], axis=1)
     c_block, x_recv = lax.optimization_barrier((c_block, x_recv))
     c_recv = lax.all_to_all(spread(c_block), EXPERT_AXES, 0, 0, tiled=True)
     cot_recv = c_recv[:, :half].reshape(row_total, width)

time: 276 us -> 297 us (1.076)
  waiting for transfers between devices: 89.4 us -> 105 us
  local copies, waits for them, and re-layouts: 16.1 us -> 23.6 us
    ppermute x0 -> x3, waiting for transfers between devices: none -> 52 us  [per_device(): lax.ppermute(moving, 'section', [(i, (i + 1) % peers) for i in range(peer...]
    all_gather x1 -> x0, waiting for transfers between devices: 34.7 us -> none  [per_device(): x_rows = lax.all_gather(x_recv, 'section', axis=1, tiled=True)]
    unnamed x23 -> x34, local copies, waits for them, and re-layouts: 0.95 us -> 8.18 us
  transfers between devices with their start and end apart: 7 -> 9, of which waited for: 5 -> 7; matrix products, arithmetic and copies ran while one was open for 9% -> 9% of each run, Pallas kernels for 0% -> 0%
where the time goes in v1:
time: 297 us; the launch traced here: 296 us
  waiting for transfers between devices  105 us (35%)
  blocking collectives  92 us (31%)
  matrix products  30.1 us (10%)
  starting transfers between devices  27.9 us (9%)
  local copies, waits for them, and re-layouts  23.6 us (8%)
  between operations  14.1 us (5%)
  other arithmetic  3.15 us (1%)
    ppermute x3, waiting for transfers between devices, per_device(): lax.ppermute(moving, 'section', [(i, (i + 1) % peers) for i in range(peer...  52 us
    all_to_all x1, blocking collectives, per_device(): x_recv = lax.all_to_all(spread(x_block), EXPERT_AXES, 0, 0, tiled=True)  35.9 us
    all_gather x2, blocking collectives, per_device(): router_part = jnp.sum(lax.all_gather(router_part, name, axis=0), axis=0)  31 us
    all_to_all x1, waiting for transfers between devices, per_device(): lax.all_to_all(out_red.reshape(n_dev, half, LANES), EXPERT_AXES, 0, 0, ti...  22.9 us
    all_to_all x1, waiting for transfers between devices, per_device(): c_recv = lax.all_to_all(spread(c_block), EXPERT_AXES, 0, 0, tiled=True)  14.8 us
    psum x1, blocking collectives, per_device(): lax.psum(jnp.dot(x_recv, w_router, preferred_element_type=jnp.float32), '...  13.1 us
    all_to_all x1, waiting for transfers between devices, per_device(): lax.all_to_all(dx_red.reshape(n_dev, half, LANES), EXPERT_AXES, 0, 0, til...  11.1 us
    all_to_all x1, starting transfers between devices, per_device(): lax.all_to_all(dx_red.reshape(n_dev, half, LANES), EXPERT_AXES, 0, 0, til...  10.6 us
  transfers between devices with their start and end apart: 9, of which 7 were waited for; matrix products, arithmetic and copies ran while one was open for 9% of the time, Pallas kernels for 0%

profile of v1, /device:TPU:1, one launch (start us, length us, event | category | flops | bytes accessed | tf_op | source)
XLA Modules:
  0.0 296.1 jit_solution(17639754391339470567)
XLA Ops:
  7.2 0.9 copy.41
  8.7 0.7 multiply_add_fusion
  9.4 0.8 slice_bitcast_fusion.3
  10.2 1.0 convolution_convert_fusion.5
  11.4 35.9 %all_to_all.20 = bf16[64,48,128]{2,1,0:T(8,128)(2,1)} all-to-all(bf16[64,48,128]{2,1,0:T(8,128)(2,1)S(1)} %bitcast.98), channel_id=1, replica_groups=mesh['section'=4,'ex'=4,'ez'=8,'ec'=2] {'ex','ez','ec'}, dimensions={0} | all-to-all | bytes 1572864 | tf_op jit(solution)/shard_map/all_to_all | solution.py:58
  47.2 1.4 reshape.137
  48.7 1.4 collective-permute-start
  50.0 18.8 %collective-permute-done = bf16[384,1024]{1,0:T(8,128)(2,1)S(1)} collective-permute-done((bf16[384,1024]{1,0:T(8,128)(2,1)S(1)}, bf16[384,1024]{1,0:T(8,128)(2,1)S(1)}, u32[]{:S(2)}, u32[]{:S(2)}) %collective-permute-start) | collective-permute-done | bytes 786464 | tf_op jit(solution)/shard_map/ppermute | solution.py:68
  68.8 0.9 copy-done.3
  69.7 19.2 %collective-permute-done.1 = bf16[384,1024]{1,0:T(8,128)(2,1)} collective-permute-done((bf16[384,1024]{1,0:T(8,128)(2,1)S(1)}, bf16[384,1024]{1,0:T(8,128)(2,1)}, u32[]{:S(2)}, u32[]{:S(2)}) %collective-permute-start.1) | collective-permute-done | bytes 786464 | tf_op jit(solution)/shard_map/ppermute | solution.py:68
  88.9 4.5 %reshape_squeeze.9 = bf16[256,4,1024]{2,1,0:T(4,128)(2,1)} reshape(bf16[1,256,4096]{2,1,0:T(8,128)(2,1)} %param.15) | data formatting | bytes 4194304 | tf_op jit(solution)/shard_map/reshape;squeeze | solution.py:98
  93.4 14.0 %collective-permute-done.2 = bf16[384,1024]{1,0:T(8,128)(2,1)} collective-permute-done((bf16[384,1024]{1,0:T(8,128)(2,1)}, bf16[384,1024]{1,0:T(8,128)(2,1)}, u32[]{:S(2)}, u32[]{:S(2)}) %collective-permute-start.2) | collective-permute-done | bytes 786464 | tf_op jit(solution)/shard_map/ppermute | solution.py:68
  107.4 1.2 constant_dynamic-update-slice_fusion.7
  108.6 1.2 constant_dynamic-update-slice_fusion.6
  109.9 1.3 constant_dynamic-update-slice_fusion.3
  111.3 1.2 constant_dynamic-update-slice_fusion.2
  112.6 1.0 fusion.7
  113.7 1.7 multiply_convert_fusion.5
  115.7 1.0 copy-done.1
  116.7 3.4 %convolution_convert_fusion.3 = bf16[384,4,1024]{2,0,1:T(8,128)(2,1)} fusion(bf16[256,4,1024]{2,1,0:T(4,128)(2,1)S(1)} %copy-done.1, bf16[384,256]{1,0:T(8,128)(2,1)S(1)} %get-tuple-element.59), kind=kOutput, calls=%fused_computation.8 | convolution fusion | flops 806879232 | bytes 5439488 | tf_op jit(solution)/shard_map/pf,fsd->spd/dot_general | solution.py:101
  120.7 1.2 broadcast_in_dim.104
  121.9 9.6 %all-to-all-start.1 = ((bf16[64,64,128]{2,1,0:T(8,128)(2,1)}), bf16[64,64,128]{2,1,0:T(8,128)(2,1)}, u32[]{:S(2)}, u32[]{:S(2)}) async-start(bf16[64,64,128]{2,1,0:T(8,128)(2,1)} %bitcast.97), calls=%async_computation.2 | async-start | bytes 2097152 | tf_op jit(solution)/shard_map/all_to_all | solution.py:73
  131.8 0.3 fusion.44
  132.1 13.1 %all-reduce.1 = (f32[384,8]{0,1:T(8,128)S(1)}, f32[16,8]{0,1:T(8,128)S(1)}) all-reduce(f32[384,8]{0,1:T(8,128)S(1)} %fusion.44, f32[16,8]{0,1:T(8,128)S(1)} %convolution_bitcast_fusion.1), channel_id=1, replica_groups=mesh['section'=4,'ex'=4,'ez'=8,'ec'=2] {'section'}, use_global_device_ids=true, to_apply=%region_4.5 | all-reduce | flops 3200 | bytes 25600 | tf_op jit(solution)/shard_map/psum | solution.py:83
  145.2 14.8 %all-to-all-done.1 = bf16[64,64,128]{2,1,0:T(8,128)(2,1)} async-done(((bf16[64,64,128]{2,1,0:T(8,128)(2,1)}), bf16[64,64,128]{2,1,0:T(8,128)(2,1)}, u32[]{:S(2)}, u32[]{:S(2)}) %all-to-all-start.1) | async-done | bytes 1048608 | tf_op jit(solution)/shard_map/all_to_all | solution.py:73
  160.0 1.0 fusion.24
  161.2 1.2 slice.73
  162.4 1.2 reshape.141
  163.7 2.2 reshape.142
  165.9 6.2 %all-to-all-start.2 = ((bf16[64,48,128]{2,1,0:T(8,128)(2,1)}), bf16[64,48,128]{2,1,0:T(8,128)(2,1)S(1)}, u32[]{:S(2)}, u32[]{:S(2)}) async-start(bf16[64,48,128]{2,1,0:T(8,128)(2,1)} %reshape.142), calls=%async_computation.3 | async-start | bytes 1572864 | tf_op jit(solution)/shard_map/all_to_all | solution.py:110
  172.1 22.9 %all-to-all-done.2 = bf16[64,48,128]{2,1,0:T(8,128)(2,1)S(1)} async-done(((bf16[64,48,128]{2,1,0:T(8,128)(2,1)}), bf16[64,48,128]{2,1,0:T(8,128)(2,1)S(1)}, u32[]{:S(2)}, u32[]{:S(2)}) %all-to-all-start.2) | async-done | bytes 786464 | tf_op jit(solution)/shard_map/all_to_all | solution.py:110
  195.4 1.0 fusion.22
  196.4 7.0 %psum.30 = f32[16,2]{0,1:T(2,128)S(1)} all-reduce(f32[16,2]{0,1:T(2,128)S(1)} %pad_maximum_fusion), channel_id=1, replica_groups=mesh['section'=4,'ex'=4,'ez'=8,'ec'=2] {'section'}, use_global_device_ids=true, to_apply=%region_12.13 | all-reduce | flops 32 | bytes 256 | tf_op jit(solution)/shard_map/psum | solution.py:143
  203.5 3.9 %multiply_convert_fusion.3 = (bf16[384,256]{1,0:T(8,128)(2,1)S(1)}, bf16[384,256]{1,0:T(8,128)(2,1)S(1)}) fusion(f32[384,256]{1,0:T(8,128)} %copy-done.12, f32[384,256]{1,0:T(8,128)} %get-tuple-element.60, bf16[1,256,4096]{2,1,0:T(8,128)(2,1)} %param.15, bf16[384,4096]{1,0:T(8,128)(2,1)} %all-gather.3.cloned.1.call-done, f32[384]{0:T(512)S(1)} %add_divide_fusion.1), kind=kOutput, calls=%fused_computation.29 | convolution fusion | flops 811302912 | bytes 6424064 | tf_op jit(solution)/shard_map/pd,fd->pf/dot_general | solution.py:113
  207.4 1.0 fusion.18
  208.4 2.8 add_convert_fusion
  211.4 5.0 %psum.31 = f32[1,8,1024]{2,1,0:T(8,128)S(1)} all-reduce(f32[1,8,1024]{2,1,0:T(8,128)S(1)} %convolution_bitcast_fusion), channel_id=1, replica_groups=mesh['section'=4,'ex'=4,'ez'=8,'ec'=2] {'ec'}, use_global_device_ids=true, to_apply=%region_13.14 | all-reduce | flops 8192 | bytes 65536 | tf_op jit(solution)/shard_map/psum | solution.py:152
  216.4 20.2 %all_gather.17 = f32[8,8,1024]{2,1,0:T(8,128)S(1)} all-gather(f32[1,8,1024]{2,1,0:T(8,128)S(1)} %psum.31), channel_id=1, replica_groups=mesh['section'=4,'ex'=4,'ez'=8,'ec'=2] {'ez'}, dimensions={0}, use_global_device_ids=true | all-gather | bytes 294912 | tf_op jit(solution)/shard_map/all_gather | solution.py:154
  236.7 10.8 %all-gather = f32[32,1024]{1,0:T(8,128)S(1)} all-gather(f32[8,1024]{1,0:T(8,128)S(1)} %reduce_sum.107), channel_id=2, replica_groups=mesh['section'=4,'ex'=4,'ez'=8,'ec'=2] {'ex'}, dimensions={0}, use_global_device_ids=true | all-gather | bytes 163840 | tf_op jit(solution)/shard_map/all_gather | solution.py:154
  247.4 0.6 bitcast_reduce_fusion
  248.1 4.2 %reduce-scatter.5.cloned.1.call-done = bf16[384,1024]{1,0:T(8,128)(2,1)} async-done(((bf16[1536,1024]{1,0:T(8,128)(2,1)}), bf16[384,1024]{1,0:T(8,128)(2,1)}) %reduce-scatter.5.cloned.1.call-update) | async-done | bytes 786448 | tf_op jit(solution)/shard_map/reduce_scatter | solution.py:150
  252.3 2.2 reshape.145
  254.5 10.6 %all-to-all-start.3 = ((bf16[64,48,128]{2,1,0:T(8,128)(2,1)}), bf16[64,48,128]{2,1,0:T(8,128)(2,1)S(1)}, u32[]{:S(2)}, u32[]{:S(2)}) async-start(bf16[64,48,128]{2,1,0:T(8,128)(2,1)} %reshape.145), calls=%async_computation.5 | async-start | bytes 1572864 | tf_op jit(solution)/shard_map/all_to_all | solution.py:156
  265.1 4.5 %fusion.1 = bf16[1,4096,256]{2,1,0:T(8,128)(2,1)} fusion(bf16[384,256]{1,0:T(8,128)(2,1)S(1)} %get-tuple-element.50, bf16[384,8192]{1,0:T(8,128)(2,1)} %copy-done.10, s32[]{:T(128)S(6)} %select_n.44), kind=kOutput, calls=%fused_computation.6 | convolution fusion | flops 806354944 | bytes 5439492 | tf_op jit(solution)/shard_map/pd,pf->df/dot_general | solution.py:124
  269.6 4.7 %fusion = bf16[1,4096,256]{2,1,0:T(8,128)(2,1)} fusion(bf16[384,256]{1,0:T(8,128)(2,1)S(1)} %get-tuple-element.51, bf16[384,8192]{1,0:T(8,128)(2,1)} %copy-done.10, s32[]{:T(128)S(6)} %select_n.44), kind=kOutput, calls=%fused_computation.5 | convolution fusion | flops 806354944 | bytes 5439492 | tf_op jit(solution)/shard_map/pd,pf->df/dot_general | solution.py:121
  274.3 2.7 fusion.2
  277.0 11.1 %all-to-all-done.3 = bf16[64,48,128]{2,1,0:T(8,128)(2,1)S(1)} async-done(((bf16[64,48,128]{2,1,0:T(8,128)(2,1)}), bf16[64,48,128]{2,1,0:T(8,128)(2,1)S(1)}, u32[]{:S(2)}, u32[]{:S(2)}) %all-to-all-start.3) | async-done | bytes 786464 | tf_op jit(solution)/shard_map/all_to_all | solution.py:156
  288.7 0.8 fusion.14
  (72 shorter events, 3.5 us)
Async XLA Ops:
  7.2 106.5 %copy-start = (bf16[1,4096,256]{2,1,0:T(8,128)(2,1)S(1)}, bf16[1,4096,256]{2,1,0:T(8,128)(2,1)}, u32[]{:S(2)}) copy-start(bf16[1,4096,256]{2,1,0:T(8,128)(2,1)} %param.14) | copy-start | bytes 6291460
  7.2 156.5 %reduce-scatter.3.cloned.1.call-start = ((), (), s32[]{:S(2)}) async-start(), calls=%async_computation.6 | async-start | bytes 3932160 | tf_op jit(solution)/shard_map/reduce_scatter | solution.py:103
  48.7 20.1 %collective-permute-start = (bf16[384,1024]{1,0:T(8,128)(2,1)S(1)}, bf16[384,1024]{1,0:T(8,128)(2,1)S(1)}, u32[]{:S(2)}, u32[]{:S(2)}) collective-permute-start(bf16[384,1024]{1,0:T(8,128)(2,1)S(1)} %reshape.137), channel_id=1, source_target_pairs={{0,64},{64,128},{128,192},{192,0},{1,65},{65,129},{129,193},{193,1... | collective-permute-start | bytes 2359304 | tf_op jit(solution)/shard_map/ppermute | solution.py:68
  68.8 0.9 copy-start.3
  69.7 19.2 %collective-permute-start.1 = (bf16[384,1024]{1,0:T(8,128)(2,1)S(1)}, bf16[384,1024]{1,0:T(8,128)(2,1)}, u32[]{:S(2)}, u32[]{:S(2)}) collective-permute-start(bf16[384,1024]{1,0:T(8,128)(2,1)S(1)} %collective-permute-done), channel_id=1, source_target_pairs={{0,64},{64,128},{128,192},{192,0},{1,65},{65,129},{129,193},{193,1... | collective-permute-start | bytes 2359304 | tf_op jit(solution)/shard_map/ppermute | solution.py:68
  88.9 18.5 %collective-permute-start.2 = (bf16[384,1024]{1,0:T(8,128)(2,1)}, bf16[384,1024]{1,0:T(8,128)(2,1)}, u32[]{:S(2)}, u32[]{:S(2)}) collective-permute-start(bf16[384,1024]{1,0:T(8,128)(2,1)} %collective-permute-done.1), channel_id=1, source_target_pairs={{0,64},{64,128},{128,192},{192,0},{1,65},{65,129},{129,193},{193,1... | collective-permute-start | bytes 2359304 | tf_op jit(solution)/shard_map/ppermute | solution.py:68
  93.4 16.4 %copy-start.4 = (bf16[384,1024]{1,0:T(8,128)(2,1)S(1)}, bf16[384,1024]{1,0:T(8,128)(2,1)}, u32[]{:S(2)}) copy-start(bf16[384,1024]{1,0:T(8,128)(2,1)} %copy-done.3) | copy-start | bytes 2359300
  109.9 2.7 copy-start.5
  112.6 2.8 copy-start.10
  113.7 2.0 copy-start.12
  113.7 3.0 %copy-start.1 = (bf16[256,4,1024]{2,1,0:T(4,128)(2,1)S(1)}, bf16[256,4,1024]{2,1,0:T(4,128)(2,1)}, u32[]{:S(2)}) copy-start(bf16[256,4,1024]{2,1,0:T(4,128)(2,1)} %reshape_squeeze.9) | copy-start | bytes 6291460
  116.7 3.6 %copy-start.9 = (bf16[16,1024]{1,0:T(8,128)(2,1)S(1)}, bf16[16,1024]{1,0:T(8,128)(2,1)}, u32[]{:S(2)}) copy-start(bf16[16,1024]{1,0:T(8,128)(2,1)} %param.10) | copy-start | bytes 98308
  120.1 11.6 %copy-start.7 = (bf16[16,1024]{1,0:T(8,128)(2,1)S(1)}, bf16[16,1024]{1,0:T(8,128)(2,1)}, u32[]{:S(2)}) copy-start(bf16[16,1024]{1,0:T(8,128)(2,1)} %param.9) | copy-start | bytes 98308
  120.1 11.6 %copy-start.8 = (bf16[1024,8]{0,1:T(8,128)(2,1)S(1)}, bf16[1024,8]{0,1:T(8,128)(2,1)}, u32[]{:S(2)}) copy-start(bf16[1024,8]{0,1:T(8,128)(2,1)} %param.12) | copy-start | bytes 49156
  120.1 25.0 %copy-start.11 = (s32[16,2]{0,1:T(2,128)S(1)}, s32[16,2]{0,1:T(2,128)}, u32[]{:S(2)}) copy-start(s32[16,2]{0,1:T(2,128)} %param.11) | copy-start | bytes 388
  121.9 38.1 %all-to-all-start.1 = ((bf16[64,64,128]{2,1,0:T(8,128)(2,1)}), bf16[64,64,128]{2,1,0:T(8,128)(2,1)}, u32[]{:S(2)}, u32[]{:S(2)}) async-start(bf16[64,64,128]{2,1,0:T(8,128)(2,1)} %bitcast.97), calls=%async_computation.2 | async-start | bytes 2097152 | tf_op jit(solution)/shard_map/all_to_all | solution.py:73
  131.6 71.9 %all-gather.3.cloned.1.call-start = ((), (), s32[]{:S(2)}) async-start(), calls=%async_computation.7 | async-start | bytes 3932160 | tf_op jit(solution)/shard_map/all_gather | solution.py:107
  165.9 29.2 %all-to-all-start.2 = ((bf16[64,48,128]{2,1,0:T(8,128)(2,1)}), bf16[64,48,128]{2,1,0:T(8,128)(2,1)S(1)}, u32[]{:S(2)}, u32[]{:S(2)}) async-start(bf16[64,48,128]{2,1,0:T(8,128)(2,1)} %reshape.142), calls=%async_computation.3 | async-start | bytes 1572864 | tf_op jit(solution)/shard_map/all_to_all | solution.py:110
  172.1 80.2 %reduce-scatter.5.cloned.1.call-start = ((), (), s32[]{:S(2)}) async-start(), calls=%async_computation.8 | async-start | bytes 3932160 | tf_op jit(solution)/shard_map/reduce_scatter | solution.py:150
  203.5 3.9 %copy-start.6 = (bf16[1,4096,256]{2,1,0:T(8,128)(2,1)S(1)}, bf16[1,4096,256]{2,1,0:T(8,128)(2,1)}, u32[]{:S(2)}) copy-start(bf16[1,4096,256]{2,1,0:T(8,128)(2,1)} %param.13) | copy-start | bytes 6291460
  254.5 33.6 %all-to-all-start.3 = ((bf16[64,48,128]{2,1,0:T(8,128)(2,1)}), bf16[64,48,128]{2,1,0:T(8,128)(2,1)S(1)}, u32[]{:S(2)}, u32[]{:S(2)}) async-start(bf16[64,48,128]{2,1,0:T(8,128)(2,1)} %reshape.145), calls=%async_computation.5 | async-start | bytes 1572864 | tf_op jit(solution)/shard_map/all_to_all | solution.py:156
  269.6 4.7 %copy-start.2 = (bf16[384,4096]{1,0:T(8,128)(2,1)S(1)}, bf16[384,4096]{1,0:T(8,128)(2,1)}, u32[]{:S(2)}) copy-start(bf16[384,4096]{1,0:T(8,128)(2,1)} %all-gather.3.cloned.1.call-done) | copy-start | bytes 9437188
Sparse Core Ops, SparseCore 0:
  120.2 39.0 reduce-scatter.2
  163.8 39.4 all-gather.2
  211.4 40.8 reduce-scatter.4
